TPU v7x, 32 devices: a whole 2x2x4 slice. The times are simulated.
32 devices in a mesh: pipe: 2 (over core), ep: 16 (over z, y, x).
Axes of the slice: x: 2, y: 2, z: 4, core: 2. Of those that a mesh axis runs over, the one named last changes fastest.
Arguments:
- x_fwd: bfloat16 [2, 1024, 2048], P('pipe', 'ep'), may hold values from -6 to 6
- ids_fwd: int32 [2, 1024, 8], P('pipe', 'ep'), may hold values from 0 to 15, all different within a row; in each aligned block of 64 rows (0 to 63, 64 to 127, ..., all dimensions but the last counted through in order) at most 48 rows name the same one
- route_fwd: float32 [2, 1024, 8], P('pipe', 'ep'), may hold values from 0.05 to 1
- x_bwd: bfloat16 [2, 1024, 2048], P('pipe', 'ep'), may hold values from -6 to 6
- grad_bwd: bfloat16 [2, 1024, 2048], P('pipe', 'ep'), may hold values from -6 to 6
- ids_bwd: int32 [2, 1024, 8], P('pipe', 'ep'), may hold values from 0 to 15, all different within a row; in each aligned block of 64 rows (0 to 63, 64 to 127, ..., all dimensions but the last counted through in order) at most 48 rows name the same one
- route_bwd: float32 [2, 1024, 8], P('pipe', 'ep'), may hold values from 0.05 to 1
- norm_gain: bfloat16 [2, 2048], P('pipe'), may hold values from 0.25 to 1.75
- w_gate: bfloat16 [2, 16, 2048, 768], P('pipe', 'ep'), may hold values from -0.125 to 0.125
- w_up: bfloat16 [2, 16, 2048, 768], P('pipe', 'ep'), may hold values from -0.125 to 0.125
- w_down: bfloat16 [2, 16, 768, 2048], P('pipe', 'ep'), may hold values from -0.21875 to 0.21875
Outputs:
- fwd_next: bfloat16 [2, 1024, 2048], P('pipe', 'ep')
- bwd_prev: bfloat16 [2, 1024, 2048], P('pipe', 'ep')
Inputs may be any that keep to these rules, and one draw needn't show every extreme that they name: `ids_fwd`: in each aligned block of 64 tokens of a section, each token names 8 different experts, no expert is named by more than 48 tokens, and in some block one expert is named by exactly 48. `ids_bwd`: as for ids_fwd.
All inputs are finite; a program needn't handle non-finite values.
Results may differ from a plain program's by a relative error of at most 0.0046.
Values may be sent and summed in bfloat16 or wider, within the bound.
No kernel may reach another device: no remote copies, remote signals or barrier semaphores. Data moves between devices by JAX's collectives and lax.ppermute only.
A program may use at most 128 MiB of HBM per device.

v0:
```python
import jax
import jax.numpy as jnp
from jax import lax
from jax.sharding import PartitionSpec as P

EPS = 1e-06


def from_behind(block, axis, distance):
    devices = range(lax.axis_size(axis))
    route = [((i - distance) % len(devices), i) for i in devices]
    return lax.ppermute(block, axis, route)


def slot_places(ids, n_exp, cap):
    flat = ids.reshape(-1)
    onehot = (flat[:, None] == jnp.arange(n_exp, dtype=jnp.int32)[None, :]).astype(jnp.int32)
    before = jnp.cumsum(onehot, axis=0) - onehot
    slot = jnp.sum(before * onehot, axis=1)
    return flat * cap + slot


def rms_stats(x):
    xf = x.astype(jnp.float32)
    scale = lax.rsqrt(jnp.mean(xf * xf, axis=-1, keepdims=True) + EPS)
    return (xf, scale)


def expert_forward(rows, w_g, w_u, w_d):
    gate = jnp.dot(rows, w_g, preferred_element_type=jnp.float32)
    upper = jnp.dot(rows, w_u, preferred_element_type=jnp.float32)
    act = (jax.nn.silu(gate) * upper).astype(jnp.bfloat16)
    return jnp.dot(act, w_d, preferred_element_type=jnp.float32).astype(jnp.bfloat16)


def expert_backward(rows, cot, w_g, w_u, w_d):
    gate = jnp.dot(rows, w_g, preferred_element_type=jnp.float32)
    upper = jnp.dot(rows, w_u, preferred_element_type=jnp.float32)
    sigma = jax.nn.sigmoid(gate)
    dact = jnp.dot(cot, w_d.T, preferred_element_type=jnp.float32)
    dgate = (dact * upper * sigma * (1.0 + gate * (1.0 - sigma))).astype(jnp.bfloat16)
    dup = (dact * gate * sigma).astype(jnp.bfloat16)
    total = jnp.dot(dgate, w_g.T, preferred_element_type=jnp.float32) + jnp.dot(
        dup, w_u.T, preferred_element_type=jnp.float32
    )
    return total.astype(jnp.bfloat16)


def norm_backward(xf, scale, gain, upstream):
    scaled = gain * upstream
    inner = jnp.mean(xf * scaled, axis=-1, keepdims=True)
    return scale * scaled - xf * (scale * scale * scale) * inner


def expert_slots(ids_all, weights_all, me, cap):
    match = ids_all == me
    chosen = jnp.any(match, axis=-1)
    weight = jnp.sum(jnp.where(match, weights_all, 0.0), axis=-1)
    pos = jnp.cumsum(chosen.astype(jnp.int32), axis=1) - chosen.astype(jnp.int32)
    slot = jnp.arange(cap, dtype=jnp.int32)[None, :, None]
    onehot = chosen[:, None, :] & (pos[:, None, :] == slot)
    slot_w = jnp.sum(jnp.where(onehot, weight[:, None, :], 0.0), axis=-1)
    return (onehot.astype(jnp.bfloat16), slot_w)


def pick_rows(onehot, rows):
    picked = jnp.einsum("bct,btd->bcd", onehot, rows, preferred_element_type=jnp.float32)
    return picked.astype(jnp.bfloat16)


def combine_rows(places, back, top):
    count = back.shape[0]
    onehot = (places[:, None] == jnp.arange(count, dtype=jnp.int32)[None, :]).astype(jnp.bfloat16)
    picked = jnp.dot(onehot, back, preferred_element_type=jnp.float32)
    return picked.reshape(-1, top, back.shape[1])


def _pairs(n, n2, stage, move):
    out = []
    for i in range(n):
        e1, e2 = (i // n2, i % n2)
        if stage == 1:
            e1 = move(e1)
        else:
            e2 = move(e2)
        out.append((i, e1 * n2 + e2))
    return out


def gather_ep(v, axis_name):
    n = lax.axis_size(axis_name)
    n2 = 4
    if n % n2 or v.shape[0] % 2:
        return lax.all_gather(v, axis_name, axis=0, tiled=False)
    n1 = n // n2
    me = lax.axis_index(axis_name)
    e1, e2 = (me // n2, me % n2)
    s1 = jnp.zeros((n1,) + v.shape, v.dtype)
    s1 = lax.dynamic_update_index_in_dim(s1, v, e1, 0)
    for d in range(1, n1):
        got = lax.ppermute(v, axis_name, _pairs(n, n2, 1, lambda a: (a + d) % n1))
        s1 = lax.dynamic_update_index_in_dim(s1, got, (e1 - d) % n1, 0)
    flip_x = lambda a: a ^ 1
    flip_y = lambda a: a ^ 2
    px = lax.ppermute(s1, axis_name, _pairs(n, n2, 2, flip_x))
    py = lax.ppermute(s1, axis_name, _pairs(n, n2, 2, flip_y))
    h = v.shape[0] // 2
    d1 = lax.ppermute(px[:, :h], axis_name, _pairs(n, n2, 2, flip_y))
    d2 = lax.ppermute(py[:, h:], axis_name, _pairs(n, n2, 2, flip_x))
    diag = jnp.concatenate([d1, d2], axis=1)
    s2 = jnp.zeros((n2,) + s1.shape, v.dtype)
    s2 = lax.dynamic_update_index_in_dim(s2, s1, e2, 0)
    s2 = lax.dynamic_update_index_in_dim(s2, px, e2 ^ 1, 0)
    s2 = lax.dynamic_update_index_in_dim(s2, py, e2 ^ 2, 0)
    s2 = lax.dynamic_update_index_in_dim(s2, diag, e2 ^ 3, 0)
    return jnp.swapaxes(s2, 0, 1).reshape((n,) + v.shape)


def local(
    x_fwd, ids_fwd, route_fwd, x_bwd, grad_bwd, ids_bwd, route_bwd, norm_gain, w_gate, w_up, w_down
):
    n_exp = lax.axis_size("ep")
    me = lax.axis_index("ep")
    tok_dev = x_fwd.shape[1]
    width = x_fwd.shape[2]
    top = ids_fwd.shape[2]
    cap = 3 * tok_dev * top // (2 * n_exp)
    gain = norm_gain[0].astype(jnp.float32)
    w_g = w_gate[0, 0]
    w_u = w_up[0, 0]
    w_d = w_down[0, 0]
    xf, scale_f = rms_stats(x_fwd[0])
    h_f = (xf * scale_f * gain).astype(jnp.bfloat16)
    xb, scale_b = rms_stats(x_bwd[0])
    h_b = (xb * scale_b * gain).astype(jnp.bfloat16)
    grad = grad_bwd[0]
    weights_f = route_fwd[0] / jnp.sum(route_fwd[0], axis=-1, keepdims=True)
    weights_b = route_bwd[0] / jnp.sum(route_bwd[0], axis=-1, keepdims=True)

    def split3(r):
        hi = lax.reduce_precision(r, exponent_bits=8, mantissa_bits=7)
        rest = r - hi
        mid = lax.reduce_precision(rest, exponent_bits=8, mantissa_bits=7)
        return jnp.concatenate([hi, mid, rest - mid], axis=-1).astype(jnp.bfloat16)

    def join3(p):
        p = p.astype(jnp.float32)
        return p[..., 0:top] + p[..., top : 2 * top] + p[..., 2 * top : 3 * top]

    meta = jnp.concatenate(
        [
            ids_fwd[0].astype(jnp.bfloat16),
            ids_bwd[0].astype(jnp.bfloat16),
            split3(route_fwd[0]),
            split3(route_bwd[0]),
        ],
        axis=-1,
    )
    pad = -meta.shape[-1] % 128
    meta = jnp.concatenate([meta, jnp.zeros((tok_dev, pad), jnp.bfloat16)], axis=-1)
    message = gather_ep(jnp.concatenate([h_f, h_b, grad, meta], axis=-1), "ep")
    all_h_f = message[..., 0:width]
    all_h_b = message[..., width : 2 * width]
    all_g = message[..., 2 * width : 3 * width]
    got = message[..., 3 * width :]
    all_ids_f = got[..., 0:top].astype(jnp.int32)
    all_ids_b = got[..., top : 2 * top].astype(jnp.int32)
    all_route_f = join3(got[..., 2 * top : 5 * top])
    all_route_b = join3(got[..., 5 * top : 8 * top])
    all_w_f = all_route_f / jnp.sum(all_route_f, axis=-1, keepdims=True)
    all_w_b = all_route_b / jnp.sum(all_route_b, axis=-1, keepdims=True)
    onehot_f, _ = expert_slots(all_ids_f, all_w_f, me, cap)
    rows = pick_rows(onehot_f, all_h_f).reshape(-1, width)
    made_f = expert_forward(rows, w_g, w_u, w_d).reshape(n_exp, cap, width)
    back_f = lax.all_to_all(made_f, "ep", split_axis=0, concat_axis=0, tiled=True)
    onehot_b, slot_w_b = expert_slots(all_ids_b, all_w_b, me, cap)
    rows = pick_rows(onehot_b, all_h_b).reshape(-1, width)
    g_rows = pick_rows(onehot_b, all_g)
    cots = (
        (slot_w_b[:, :, None] * g_rows.astype(jnp.float32)).astype(jnp.bfloat16).reshape(-1, width)
    )
    made_b = expert_backward(rows, cots, w_g, w_u, w_d).reshape(n_exp, cap, width)
    back_b = lax.all_to_all(made_b, "ep", split_axis=0, concat_axis=0, tiled=True)
    places_f = slot_places(ids_fwd[0], n_exp, cap)
    picked_f = combine_rows(places_f, back_f.reshape(-1, width), top)
    mixed = jnp.sum(weights_f[:, :, None] * picked_f, axis=1)
    layer_out = (xf + mixed).astype(jnp.bfloat16)[None]
    places_b = slot_places(ids_bwd[0], n_exp, cap)
    picked_b = combine_rows(places_b, back_b.reshape(-1, width), top)
    dnorm = jnp.sum(picked_b, axis=1)
    input_grad = (grad.astype(jnp.float32) + norm_backward(xb, scale_b, gain, dnorm)).astype(
        jnp.bfloat16
    )[None]
    fwd_next = from_behind(layer_out, "pipe", 1)
    bwd_prev = from_behind(input_grad, "pipe", -1)
    return (fwd_next, bwd_prev)


def solution(mesh):
    placed = (
        P("pipe", "ep", None),
        P("pipe", "ep", None),
        P("pipe", "ep", None),
        P("pipe", "ep", None),
        P("pipe", "ep", None),
        P("pipe", "ep", None),
        P("pipe", "ep", None),
        P("pipe", None),
        P("pipe", "ep", None, None),
        P("pipe", "ep", None, None),
        P("pipe", "ep", None, None),
    )
    return jax.shard_map(
        local,
        mesh=mesh,
        in_specs=placed,
        out_specs=(P("pipe", "ep", None), P("pipe", "ep", None)),
        check_vma=False,
    )
```

profile of v0, /device:TPU:13, one launch (start us, length us, event | category | flops | bytes accessed | tf_op | source)
XLA Modules:
  0.0 404.9 jit_solution(13965254821809151938)
XLA Ops:
  12.8 2.0 concatenate.11
  18.6 1.9 broadcast_in_dim.77
  21.5 12.4 %collective-permute-done = bf16[64,6272]{1,0:T(8,128)(2,1)} collective-permute-done((bf16[64,6272]{1,0:T(8,128)(2,1)}, bf16[64,6272]{1,0:T(8,128)(2,1)}, u32[]{:S(2)}, u32[]{:S(2)}) %collective-permute-start) | collective-permute-done | bytes 802848 | tf_op jit(solution)/shard_map/ppermute | solution.py:101
  33.9 2.1 bitcast_dynamic-update-slice_fusion.5
  36.0 48.6 %collective-permute-done.1 = bf16[64,6272]{1,0:T(8,128)(2,1)} collective-permute-done((bf16[64,6272]{1,0:T(8,128)(2,1)}, bf16[64,6272]{1,0:T(8,128)(2,1)}, u32[]{:S(2)}, u32[]{:S(2)}) %collective-permute-start.1) | collective-permute-done | bytes 802848 | tf_op jit(solution)/shard_map/ppermute | solution.py:101
  84.6 2.1 bitcast_dynamic-update-slice_fusion.4
  87.5 2.1 bitcast_dynamic-update-slice_fusion.3
  91.0 6.2 %broadcast_in_dim.76 = bf16[4,4,64,6272]{3,2,0,1:T(8,128)(2,1)} broadcast(bf16[]{:T(256)} %constant.89.clone.1), dimensions={} | broadcast | bytes 12845058 | tf_op jit(solution)/shard_map/broadcast_in_dim | solution.py:111
  97.2 3.8 bitcast_dynamic-update-slice_fusion.2
  101.0 59.1 %collective-permute-done.3 = bf16[4,64,6272]{2,1,0:T(8,128)(2,1)} collective-permute-done((bf16[4,64,6272]{2,1,0:T(8,128)(2,1)}, bf16[4,64,6272]{2,1,0:T(8,128)(2,1)}, u32[]{:S(2)}, u32[]{:S(2)}) %collective-permute-start.3) | collective-permute-done | bytes 3211296 | tf_op jit(solution)/shard_map/ppermute | solution.py:105
  164.7 3.8 bitcast_dynamic-update-slice_fusion.1
  168.6 3.8 bitcast_dynamic-update-slice_fusion
  172.4 24.3 %collective-permute-done.5 = bf16[4,32,6272]{2,1,0:T(8,128)(2,1)S(1)} collective-permute-done((bf16[4,32,6272]{2,1,0:T(8,128)(2,1)S(1)}, bf16[4,32,6272]{2,1,0:T(8,128)(2,1)S(1)}, u32[]{:S(2)}, u32[]{:S(2)}) %collective-permute-start.5) | collective-permute-done | bytes 1605664 | tf_op jit(solution)/shard_map/ppermute | solution.py:108
  198.2 1.9 fusion.16
  201.3 1.9 fusion.88
  203.2 6.4 %fusion.95 = f32[16,64]{1,0:T(8,128)S(1)} fusion(f32[16,64,24]{2,1,0:T(8,128)S(1)} %slice_convert_fusion, s32[]{:T(128)S(6)} %axis_index.16, bf16[16,64,6272]{2,1,0:T(8,128)(2,1)} %bitcast.179), kind=kOutput, calls=%fused_computation.135 | output fusion | flops 57351 | bytes 1593348 | tf_op jit(solution)/shard_map/div | solution.py:171
  209.8 3.1 fusion.13
  213.2 4.1 %multiply_convert_fusion = bf16[16,48,2048]{2,1,0:T(8,128)(2,1)S(1)} fusion(f32[16,48]{1,0:T(8,128)S(1)} %select_reduce_fusion, bf16[16,64,6272]{2,1,0:T(8,128)(2,1)} %bitcast.181, s32[16,64]{1,0:T(8,128)S(1)} %convert_subtract_fusion, pred[16,64]{1,0:T(8,128)(4,1)S(1)} %get-tuple-element.2), kind=kOutput, calls=%fused_computation.2 | convolution fusion | flops 207716352 | bytes 7348224 | tf_op jit(solution)/shard_map/bct,btd->bcd/dot_general | solution.py:67
  217.3 4.1 %fusion.17 = f32[768,768]{1,0:T(8,128)} fusion(bf16[768,2048]{1,0:T(8,128)(2,1)S(1)} %bitcast.189, bf16[1,1,768,2048]{3,2,1,0:T(8,128)(2,1)S(1)} %copy-done.8), kind=kOutput, calls=%fused_computation.19 | convolution fusion | flops 2415919104 | bytes 8650752 | tf_op jit(solution)/shard_map/dot_general | solution.py:40
  221.4 4.0 fusion.27
  225.5 12.9 %fusion.25 = f32[768,2048]{1,0:T(8,128)} fusion(bf16[1,1,2048,768]{3,2,1,0:T(8,128)(2,1)} %param.19, f32[768,768]{1,0:T(8,128)} %fusion.27, f32[768,768]{1,0:T(8,128)} %fusion.17, bf16[768,2048]{1,0:T(8,128)(2,1)} %bitcast.184, bf16[1,1,2048,768]{3,2,1,0:T(8,128)(2,1)S(1)} %copy-done), kind=kOutput, calls=%fused_computation.27 | convolution fusion | flops 4837736448 | bytes 20447232 | tf_op jit(solution)/shard_map/dot_general | solution.py:43
  238.3 7.4 %add_convert_fusion = bf16[768,2048]{1,0:T(8,128)(2,1)} fusion(f32[768,2048]{1,0:T(8,128)} %fusion.25, bf16[1,1,2048,768]{3,2,1,0:T(8,128)(2,1)S(1)} %copy-done, f32[768,768]{1,0:T(8,128)} %fusion.17, f32[768,768]{1,0:T(8,128)} %fusion.27), kind=kOutput, calls=%fused_computation.1 | convolution fusion | flops 2422603776 | bytes 17301504 | tf_op jit(solution)/shard_map/dot_general | solution.py:43
  245.8 5.3 %all-to-all-start.1 = ((bf16[16,48,2048]{2,1,0:T(8,128)(2,1)}), bf16[16,48,2048]{2,1,0:T(8,128)(2,1)}, u32[]{:S(2)}, u32[]{:S(2)}) async-start(bf16[16,48,2048]{2,1,0:T(8,128)(2,1)} %bitcast.188), calls=%async_computation.1 | async-start | bytes 6291456 | tf_op jit(solution)/shard_map/all_to_all | solution.py:183
  251.3 3.1 fusion.7
  256.1 4.0 fusion.23
  260.2 11.9 %convolution_convert_fusion = bf16[768,2048]{1,0:T(8,128)(2,1)} fusion(bf16[1,1,768,2048]{3,2,1,0:T(8,128)(2,1)} %param.21, f32[768,768]{1,0:T(8,128)} %fusion.23, bf16[768,2048]{1,0:T(8,128)(2,1)} %bitcast.186, bf16[1,1,2048,768]{3,2,1,0:T(8,128)(2,1)} %param.19), kind=kOutput, calls=%fused_computation.13 | convolution fusion | flops 4836950016 | bytes 14942208 | tf_op jit(solution)/shard_map/dot_general | solution.py:33
  272.0 49.7 %all-to-all-done.1 = bf16[16,48,2048]{2,1,0:T(8,128)(2,1)} async-done(((bf16[16,48,2048]{2,1,0:T(8,128)(2,1)}), bf16[16,48,2048]{2,1,0:T(8,128)(2,1)}, u32[]{:S(2)}, u32[]{:S(2)}) %all-to-all-start.1) | async-done | bytes 3145760 | tf_op jit(solution)/shard_map/all_to_all | solution.py:183
  321.8 4.6 %all-to-all-start = ((bf16[16,48,2048]{2,1,0:T(8,128)(2,1)}), bf16[16,48,2048]{2,1,0:T(8,128)(2,1)}, u32[]{:S(2)}, u32[]{:S(2)}) async-start(bf16[16,48,2048]{2,1,0:T(8,128)(2,1)} %bitcast.187), calls=%async_computation | async-start | bytes 6291456 | tf_op jit(solution)/shard_map/all_to_all | solution.py:175
  330.1 4.4 %convolution_reduce_fusion = f32[64,2048]{1,0:T(8,128)S(1)} fusion(bf16[768,2048,1]{1,0,2:T(8,128)(2,1)} %bitcast.40, s32[64,8]{1,0:T(8,128)S(1)} %bitcast_add_fusion), kind=kOutput, calls=%fused_computation.37 | convolution fusion | flops 1611923456 | bytes 3672064 | tf_op jit(solution)/shard_map/dot_general | solution.py:74
  335.7 1.9 collective-permute-start.8
  337.5 58.8 %all-to-all-done = bf16[16,48,2048]{2,1,0:T(8,128)(2,1)} async-done(((bf16[16,48,2048]{2,1,0:T(8,128)(2,1)}), bf16[16,48,2048]{2,1,0:T(8,128)(2,1)}, u32[]{:S(2)}, u32[]{:S(2)}) %all-to-all-start) | async-done | bytes 3145760 | tf_op jit(solution)/shard_map/all_to_all | solution.py:175
  396.3 4.5 %multiply_reduce_fusion = f32[64,2048]{1,0:T(8,128)S(1)} fusion(bf16[768,2048,1]{1,0,2:T(8,128)(2,1)} %bitcast.31, f32[64,8]{1,0:T(8,128)S(1)} %copy.37, s32[64,8]{1,0:T(8,128)S(1)} %bitcast_add_fusion.1), kind=kOutput, calls=%fused_computation.9 | convolution fusion | flops 1612972032 | bytes 3674112 | tf_op jit(solution)/shard_map/dot_general | solution.py:74
  (89 shorter events, 37.5 us)
Async XLA Ops:
  0.6 224.8 %copy-start = (bf16[1,1,2048,768]{3,2,1,0:T(8,128)(2,1)S(1)}, bf16[1,1,2048,768]{3,2,1,0:T(8,128)(2,1)}, u32[]{:S(2)}) copy-start(bf16[1,1,2048,768]{3,2,1,0:T(8,128)(2,1)} %param.20) | copy-start | bytes 9437188
  14.8 19.1 %collective-permute-start = (bf16[64,6272]{1,0:T(8,128)(2,1)}, bf16[64,6272]{1,0:T(8,128)(2,1)}, u32[]{:S(2)}, u32[]{:S(2)}) collective-permute-start(bf16[64,6272]{1,0:T(8,128)(2,1)} %concatenate.11), channel_id=1, source_target_pairs={{0,4},{1,5},{2,6},{3,7},{4,8},{5,9},{6,10},{7,11},{8,12},{9,13},{1... | collective-permute-start | bytes 2408456 | tf_op jit(solution)/shard_map/ppermute | solution.py:101
  16.1 68.5 %collective-permute-start.1 = (bf16[64,6272]{1,0:T(8,128)(2,1)}, bf16[64,6272]{1,0:T(8,128)(2,1)}, u32[]{:S(2)}, u32[]{:S(2)}) collective-permute-start(bf16[64,6272]{1,0:T(8,128)(2,1)} %concatenate.11), channel_id=1, source_target_pairs={{0,8},{1,9},{2,10},{3,11},{4,12},{5,13},{6,14},{7,15},{8,0},{9,1},... | collective-permute-start | bytes 2408456 | tf_op jit(solution)/shard_map/ppermute | solution.py:101
  17.2 70.3 %collective-permute-start.2 = (bf16[64,6272]{1,0:T(8,128)(2,1)}, bf16[64,6272]{1,0:T(8,128)(2,1)}, u32[]{:S(2)}, u32[]{:S(2)}) collective-permute-start(bf16[64,6272]{1,0:T(8,128)(2,1)} %concatenate.11), channel_id=1, source_target_pairs={{0,12},{1,13},{2,14},{3,15},{4,0},{5,1},{6,2},{7,3},{8,4},{9,5},{1... | collective-permute-start | bytes 2408456 | tf_op jit(solution)/shard_map/ppermute | solution.py:101
  18.6 2.0 copy-start.2
  89.5 70.6 %collective-permute-start.3 = (bf16[4,64,6272]{2,1,0:T(8,128)(2,1)}, bf16[4,64,6272]{2,1,0:T(8,128)(2,1)}, u32[]{:S(2)}, u32[]{:S(2)}) collective-permute-start(bf16[4,64,6272]{2,1,0:T(8,128)(2,1)} %bitcast_dynamic-update-slice_fusion.3), channel_id=1, source_target_pairs={{0,1},{1,0},{2,3},{3,2},{4,5},{5,4},{6,7},{7,6},{8,9},{9,8},{10,11... | collective-permute-start | bytes 9633800 | tf_op jit(solution)/shard_map/ppermute | solution.py:105
  90.7 71.2 %collective-permute-start.4 = (bf16[4,64,6272]{2,1,0:T(8,128)(2,1)}, bf16[4,64,6272]{2,1,0:T(8,128)(2,1)}, u32[]{:S(2)}, u32[]{:S(2)}) collective-permute-start(bf16[4,64,6272]{2,1,0:T(8,128)(2,1)} %bitcast_dynamic-update-slice_fusion.3), channel_id=1, source_target_pairs={{0,2},{1,3},{2,0},{3,1},{4,6},{5,7},{6,4},{7,5},{8,10},{9,11},{10,... | collective-permute-start | bytes 9633800 | tf_op jit(solution)/shard_map/ppermute | solution.py:106
  161.6 35.0 %collective-permute-start.5 = (bf16[4,32,6272]{2,1,0:T(8,128)(2,1)S(1)}, bf16[4,32,6272]{2,1,0:T(8,128)(2,1)S(1)}, u32[]{:S(2)}, u32[]{:S(2)}) collective-permute-start(bf16[4,32,6272]{2,1,0:T(8,128)(2,1)S(1)} %slice.65), channel_id=1, source_target_pairs={{0,2},{1,3},{2,0},{3,1},{4,6},{5,7},{6,4},{7,5},{8,10},{9,11},{10,... | collective-permute-start | bytes 4816904 | tf_op jit(solution)/shard_map/ppermute | solution.py:108
  163.5 34.8 %collective-permute-start.6 = (bf16[4,32,6272]{2,1,0:T(8,128)(2,1)S(1)}, bf16[4,32,6272]{2,1,0:T(8,128)(2,1)S(1)}, u32[]{:S(2)}, u32[]{:S(2)}) collective-permute-start(bf16[4,32,6272]{2,1,0:T(8,128)(2,1)S(1)} %slice.66), channel_id=1, source_target_pairs={{0,1},{1,0},{2,3},{3,2},{4,5},{5,4},{6,7},{7,6},{8,9},{9,8},{10,11... | collective-permute-start | bytes 4816904 | tf_op jit(solution)/shard_map/ppermute | solution.py:109
  213.0 8.5 %copy-start.3 = (bf16[16,48,2048]{2,1,0:T(8,128)(2,1)}, bf16[16,48,2048]{2,1,0:T(8,128)(2,1)S(1)}, u32[]{:S(2)}) copy-start(bf16[16,48,2048]{2,1,0:T(8,128)(2,1)S(1)} %fusion.13) | copy-start | bytes 9437188
  213.2 4.1 %copy-start.8 = (bf16[1,1,768,2048]{3,2,1,0:T(8,128)(2,1)S(1)}, bf16[1,1,768,2048]{3,2,1,0:T(8,128)(2,1)}, u32[]{:S(2)}) copy-start(bf16[1,1,768,2048]{3,2,1,0:T(8,128)(2,1)} %param.21) | copy-start | bytes 9437188
  217.3 4.1 %copy-start.9 = (bf16[1,1,2048,768]{3,2,1,0:T(8,128)(2,1)S(1)}, bf16[1,1,2048,768]{3,2,1,0:T(8,128)(2,1)}, u32[]{:S(2)}) copy-start(bf16[1,1,2048,768]{3,2,1,0:T(8,128)(2,1)} %param.19) | copy-start | bytes 9437188
  245.8 76.0 %all-to-all-start.1 = ((bf16[16,48,2048]{2,1,0:T(8,128)(2,1)}), bf16[16,48,2048]{2,1,0:T(8,128)(2,1)}, u32[]{:S(2)}, u32[]{:S(2)}) async-start(bf16[16,48,2048]{2,1,0:T(8,128)(2,1)} %bitcast.188), calls=%async_computation.1 | async-start | bytes 6291456 | tf_op jit(solution)/shard_map/all_to_all | solution.py:183
  254.4 1.7 copy-start.4
  321.8 74.5 %all-to-all-start = ((bf16[16,48,2048]{2,1,0:T(8,128)(2,1)}), bf16[16,48,2048]{2,1,0:T(8,128)(2,1)}, u32[]{:S(2)}, u32[]{:S(2)}) async-start(bf16[16,48,2048]{2,1,0:T(8,128)(2,1)} %bitcast.187), calls=%async_computation | async-start | bytes 6291456 | tf_op jit(solution)/shard_map/all_to_all | solution.py:175
  330.1 4.4 %copy-start.1 = (bf16[1,64,2048]{2,1,0:T(8,128)(2,1)S(1)}, bf16[1,64,2048]{2,1,0:T(8,128)(2,1)}, u32[]{:S(2)}) copy-start(bf16[1,64,2048]{2,1,0:T(8,128)(2,1)} %param.14) | copy-start | bytes 786436
  330.1 4.6 %copy-start.6 = (bf16[1,64,2048]{2,1,0:T(8,128)(2,1)S(1)}, bf16[1,64,2048]{2,1,0:T(8,128)(2,1)}, u32[]{:S(2)}) copy-start(bf16[1,64,2048]{2,1,0:T(8,128)(2,1)} %param.15) | copy-start | bytes 786436
  330.1 4.6 %copy-start.7 = (f32[64]{0:T(128)S(1)}, f32[64]{0:T(128)}, u32[]{:S(2)}) copy-start(f32[64]{0:T(128)} %get-tuple-element.13) | copy-start | bytes 772
  335.7 66.7 %collective-permute-start.8 = (bf16[1,64,2048]{2,1,0:T(8,128)(2,1)}, bf16[1,64,2048]{2,1,0:T(8,128)(2,1)S(1)}, u32[]{:S(2)}, u32[]{:S(2)}) collective-permute-start(bf16[1,64,2048]{2,1,0:T(8,128)(2,1)} %fusion.66), channel_id=1, source_target_pairs={{16,0},{0,16},{17,1},{1,17},{18,2},{2,18},{19,3},{3,19},{20,4},{4,... | collective-permute-start | bytes 786440 | tf_op jit(solution)/shard_map/ppermute | solution.py:12
  396.3 4.5 %copy-start.5 = (bf16[1,64,2048]{2,1,0:T(8,128)(2,1)S(1)}, bf16[1,64,2048]{2,1,0:T(8,128)(2,1)}, u32[]{:S(2)}) copy-start(bf16[1,64,2048]{2,1,0:T(8,128)(2,1)} %param.11) | copy-start | bytes 786436
  400.9 2.6 collective-permute-start.7
where the time goes:
time: 406 us; the launch traced here: 405 us
  waiting for transfers between devices  256 us (63%)
  matrix products  63.6 us (16%)
  local copies, waits for them, and re-layouts  40.1 us (10%)
  other arithmetic  24 us (6%)
  starting transfers between devices  20 us (5%)
    ppermute x3, waiting for transfers between devices, gather_ep(): got = lax.ppermute(v, axis_name, _pairs(n, n2, 1, lambda a: (a + d) % n1))  61.8 us
    ppermute x1, waiting for transfers between devices, gather_ep(): px = lax.ppermute(s1, axis_name, _pairs(n, n2, 2, flip_x))  59.1 us
    all_to_all x1, waiting for transfers between devices, local(): lax.all_to_all(made_f, 'ep', split_axis=0, concat_axis=0, tiled=True)  58.8 us
    all_to_all x1, waiting for transfers between devices, local(): lax.all_to_all(made_b, 'ep', split_axis=0, concat_axis=0, tiled=True)  49.7 us
    ppermute x1, waiting for transfers between devices, gather_ep(): d1 = lax.ppermute(px[:, :h], axis_name, _pairs(n, n2, 2, flip_y))  24.3 us
    dot_general x1, matrix products, expert_backward(): jnp.dot(dgate, w_g.T, preferred_element_type=jnp.float32)  12.9 us
    dot_general x1, matrix products, expert_forward(): jnp.dot(act, w_d, preferred_element_type=jnp.float32).astype(jnp.bfloat16)  11.9 us
    dot_general x3, matrix products, pick_rows(): jnp.einsum('bct,btd->bcd', onehot, rows, preferred_element_type=jnp.float32)  10.4 us
  transfers between devices with their start and end apart: 11, of which 9 were waited for; matrix products, arithmetic and copies ran while one was open for 15% of the time, Pallas kernels for 0%

commit v1 on v0

--- a/solution.py
+++ b/solution.py
@@ -4,6 +4,28 @@
 from jax.sharding import PartitionSpec as P
 
 EPS = 1e-06
+
+
+def split_up(x, dim, devices):
+    before, after = (x.shape[:dim], x.shape[dim + 1 :])
+    return jnp.moveaxis(x.reshape(*before, devices, -1, *after), dim, 0)
+
+
+def laid_out(pieces, dim):
+    dims = list(pieces.shape[1:])
+    dims[dim] *= pieces.shape[0]
+    return jnp.moveaxis(pieces, 0, dim).reshape(dims)
+
+
+def pairwise_exchange(shard, axis, split_dim, concat_dim):
+    devices, place = (lax.axis_size(axis), lax.axis_index(axis))
+    parts = split_up(shard, split_dim, devices)
+    outs = [parts[place]]
+    for step in range(1, devices):
+        sent = parts[place ^ step]
+        outs.append(lax.ppermute(sent, axis, [(i, i ^ step) for i in range(devices)]))
+    parts = jnp.stack(outs)[place ^ jnp.arange(devices)]
+    return laid_out(parts, concat_dim)
 
 
 def from_behind(block, axis, distance):
@@ -180,7 +202,7 @@
         (slot_w_b[:, :, None] * g_rows.astype(jnp.float32)).astype(jnp.bfloat16).reshape(-1, width)
     )
     made_b = expert_backward(rows, cots, w_g, w_u, w_d).reshape(n_exp, cap, width)
-    back_b = lax.all_to_all(made_b, "ep", split_axis=0, concat_axis=0, tiled=True)
+    back_b = pairwise_exchange(made_b, "ep", 0, 0)
     places_f = slot_places(ids_fwd[0], n_exp, cap)
     picked_f = combine_rows(places_f, back_f.reshape(-1, width), top)
     mixed = jnp.sum(weights_f[:, :, None] * picked_f, axis=1)

time: 406 us -> 440 us (1.084)
  starting transfers between devices: 20 us -> 46.4 us
  local copies, waits for them, and re-layouts: 40.1 us -> 61.7 us
  waiting for transfers between devices: 256 us -> 239 us
    ppermute x0 -> x15, waiting for transfers between devices: none -> 96.7 us  [pairwise_exchange(): lax.ppermute(sent, axis, [(i, i ^ step) for i in range(devices)])]
    all_to_all x1, waiting for transfers between devices: 58.8 us -> 0.01 us  [local(): lax.all_to_all(made_f, 'ep', split_axis=0, concat_axis=0, tiled=True)]
    all_to_all x1 -> x0, waiting for transfers between devices: 49.7 us -> none  [local(): lax.all_to_all(made_b, 'ep', split_axis=0, concat_axis=0, tiled=True)]
    ppermute x0 -> x15, starting transfers between devices: none -> 32.9 us  [pairwise_exchange(): lax.ppermute(sent, axis, [(i, i ^ step) for i in range(devices)])]
    unnamed x24 -> x48, local copies, waits for them, and re-layouts: 4.66 us -> 19 us
    ppermute x1, waiting for transfers between devices: 59.1 us -> 53.5 us  [gather_ep(): px = lax.ppermute(s1, axis_name, _pairs(n, n2, 2, flip_x))]
    all_to_all x1 -> x0, starting transfers between devices: 5.3 us -> none  [local(): lax.all_to_all(made_b, 'ep', split_axis=0, concat_axis=0, tiled=True)]
  transfers between devices with their start and end apart: 11 -> 25, of which waited for: 9 -> 15; matrix products, arithmetic and copies ran while one was open for 15% -> 19% of each run, Pallas kernels for 0% -> 0%
where the time goes in v1:
time: 440 us; the launch traced here: 439 us
  waiting for transfers between devices  239 us (54%)
  matrix products  62.5 us (14%)
  local copies, waits for them, and re-layouts  61.7 us (14%)
  starting transfers between devices  46.4 us (11%)
  other arithmetic  28 us (6%)
    ppermute x15, waiting for transfers between devices, pairwise_exchange(): lax.ppermute(sent, axis, [(i, i ^ step) for i in range(devices)])  96.7 us
    ppermute x3, waiting for transfers between devices, gather_ep(): got = lax.ppermute(v, axis_name, _pairs(n, n2, 1, lambda a: (a + d) % n1))  61.7 us
    ppermute x1, waiting for transfers between devices, gather_ep(): px = lax.ppermute(s1, axis_name, _pairs(n, n2, 2, flip_x))  53.5 us
    ppermute x15, starting transfers between devices, pairwise_exchange(): lax.ppermute(sent, axis, [(i, i ^ step) for i in range(devices)])  32.9 us
    ppermute x1, waiting for transfers between devices, gather_ep(): d1 = lax.ppermute(px[:, :h], axis_name, _pairs(n, n2, 2, flip_y))  24.3 us
    unnamed x48, local copies, waits for them, and re-layouts  19 us
    dot_general x1, matrix products, expert_backward(): jnp.dot(dgate, w_g.T, preferred_element_type=jnp.float32)  12.9 us
    dot_general x1, matrix products, expert_forward(): jnp.dot(act, w_d, preferred_element_type=jnp.float32).astype(jnp.bfloat16)  11.9 us
  transfers between devices with their start and end apart: 25, of which 15 were waited for; matrix products, arithmetic and copies ran while one was open for 19% of the time, Pallas kernels for 0%

profile of v1, /device:TPU:13, one launch (start us, length us, event | category | flops | bytes accessed | tf_op | source)
XLA Modules:
  0.0 438.6 jit_solution(1428492697700257810)
XLA Ops:
  21.7 12.3 %collective-permute-done = bf16[64,6272]{1,0:T(8,128)(2,1)} collective-permute-done((bf16[64,6272]{1,0:T(8,128)(2,1)}, bf16[64,6272]{1,0:T(8,128)(2,1)}, u32[]{:S(2)}, u32[]{:S(2)}) %collective-permute-start) | collective-permute-done | bytes 802848 | tf_op jit(solution)/shard_map/ppermute | solution.py:123
  36.1 48.6 %collective-permute-done.1 = bf16[64,6272]{1,0:T(8,128)(2,1)} collective-permute-done((bf16[64,6272]{1,0:T(8,128)(2,1)}, bf16[64,6272]{1,0:T(8,128)(2,1)}, u32[]{:S(2)}, u32[]{:S(2)}) %collective-permute-start.1) | collective-permute-done | bytes 802848 | tf_op jit(solution)/shard_map/ppermute | solution.py:123
  96.6 6.2 %broadcast_in_dim.77 = bf16[4,4,64,6272]{3,2,0,1:T(8,128)(2,1)} broadcast(bf16[]{:T(256)} %constant.103.clone.1), dimensions={} | broadcast | bytes 12845058 | tf_op jit(solution)/shard_map/broadcast_in_dim | solution.py:133
  102.8 3.8 bitcast_dynamic-update-slice_fusion.2
  106.7 53.5 %collective-permute-done.3 = bf16[4,64,6272]{2,1,0:T(8,128)(2,1)} collective-permute-done((bf16[4,64,6272]{2,1,0:T(8,128)(2,1)}, bf16[4,64,6272]{2,1,0:T(8,128)(2,1)}, u32[]{:S(2)}, u32[]{:S(2)}) %collective-permute-start.3) | collective-permute-done | bytes 3211296 | tf_op jit(solution)/shard_map/ppermute | solution.py:127
  164.8 3.8 bitcast_dynamic-update-slice_fusion.1
  168.6 3.8 bitcast_dynamic-update-slice_fusion
  172.5 24.3 %collective-permute-done.5 = bf16[4,32,6272]{2,1,0:T(8,128)(2,1)S(1)} collective-permute-done((bf16[4,32,6272]{2,1,0:T(8,128)(2,1)S(1)}, bf16[4,32,6272]{2,1,0:T(8,128)(2,1)S(1)}, u32[]{:S(2)}, u32[]{:S(2)}) %collective-permute-start.5) | collective-permute-done | bytes 1605664 | tf_op jit(solution)/shard_map/ppermute | solution.py:130
  203.2 6.4 %fusion.96 = f32[16,64]{1,0:T(8,128)S(1)} fusion(f32[16,64,24]{2,1,0:T(8,128)S(1)} %slice_convert_fusion, s32[]{:T(128)S(6)} %axis_index.8, bf16[16,64,6272]{2,1,0:T(8,128)(2,1)} %bitcast.242), kind=kOutput, calls=%fused_computation.170 | output fusion | flops 57351 | bytes 1593348 | tf_op jit(solution)/shard_map/div | solution.py:193
  209.9 3.1 fusion.13
  213.2 4.1 multiply_convert_fusion
  217.4 4.1 fusion.17
  221.5 4.0 fusion.27
  225.5 12.9 %fusion.25 = f32[768,2048]{1,0:T(8,128)} fusion(bf16[1,1,2048,768]{3,2,1,0:T(8,128)(2,1)} %param.19, f32[768,768]{1,0:T(8,128)} %fusion.27, f32[768,768]{1,0:T(8,128)} %fusion.17, bf16[768,2048]{1,0:T(8,128)(2,1)} %bitcast.248, bf16[1,1,2048,768]{3,2,1,0:T(8,128)(2,1)S(1)} %copy-done), kind=kOutput, calls=%fused_computation.28 | convolution fusion | flops 4837736448 | bytes 20447232 | tf_op jit(solution)/shard_map/dot_general | solution.py:65
  238.5 6.2 %add_convert_fusion = bf16[768,2048]{1,0:T(8,128)(2,1)S(1)} fusion(f32[768,2048]{1,0:T(8,128)} %fusion.25, bf16[1,1,2048,768]{3,2,1,0:T(8,128)(2,1)S(1)} %copy-done, f32[768,768]{1,0:T(8,128)} %fusion.17, f32[768,768]{1,0:T(8,128)} %fusion.27), kind=kOutput, calls=%fused_computation.2 | convolution fusion | flops 2422603776 | bytes 17301504 | tf_op jit(solution)/shard_map/dot_general | solution.py:65
  254.2 3.1 fusion.7
  259.0 4.0 fusion.23
  263.0 11.9 %convolution_convert_fusion = bf16[768,2048]{1,0:T(8,128)(2,1)} fusion(bf16[1,1,768,2048]{3,2,1,0:T(8,128)(2,1)} %param.21, f32[768,768]{1,0:T(8,128)} %fusion.23, bf16[768,2048]{1,0:T(8,128)(2,1)} %bitcast.250, bf16[1,1,2048,768]{3,2,1,0:T(8,128)(2,1)} %param.19), kind=kOutput, calls=%fused_computation.14 | convolution fusion | flops 4836950016 | bytes 14942208 | tf_op jit(solution)/shard_map/dot_general | solution.py:55
  274.9 5.2 %all-to-all-start = ((bf16[16,48,2048]{2,1,0:T(8,128)(2,1)}), bf16[16,48,2048]{2,1,0:T(8,128)(2,1)}, u32[]{:S(2)}, u32[]{:S(2)}) async-start(bf16[16,48,2048]{2,1,0:T(8,128)(2,1)} %bitcast.251), calls=%async_computation | async-start | bytes 6291456 | tf_op jit(solution)/shard_map/all_to_all | solution.py:197
  296.0 38.6 %collective-permute-done.13 = bf16[1,48,2048]{2,1,0:T(8,128)(2,1)S(1)} collective-permute-done((bf16[1,48,2048]{2,1,0:T(8,128)(2,1)}, bf16[1,48,2048]{2,1,0:T(8,128)(2,1)S(1)}, u32[]{:S(2)}, u32[]{:S(2)}) %collective-permute-start.13) | collective-permute-done | bytes 196640 | tf_op jit(solution)/shard_map/ppermute | solution.py:26
  335.3 3.0 collective-permute-done.14
  341.3 29.3 %collective-permute-done.15 = bf16[1,48,2048]{2,1,0:T(8,128)(2,1)S(1)} collective-permute-done((bf16[1,48,2048]{2,1,0:T(8,128)(2,1)}, bf16[1,48,2048]{2,1,0:T(8,128)(2,1)S(1)}, u32[]{:S(2)}, u32[]{:S(2)}) %collective-permute-start.15) | collective-permute-done | bytes 196640 | tf_op jit(solution)/shard_map/ppermute | solution.py:26
  370.6 4.3 collective-permute-start.20
  375.7 3.9 collective-permute-start.21
  381.2 9.5 %collective-permute-start.22 = (bf16[1,48,2048]{2,1,0:T(8,128)(2,1)S(1)}, bf16[1,48,2048]{2,1,0:T(8,128)(2,1)S(1)}, u32[]{:S(2)}, u32[]{:S(2)}) collective-permute-start(bf16[1,48,2048]{2,1,0:T(8,128)(2,1)S(1)} %get-tuple-element.4), channel_id=1, source_target_pairs={{0,15},{1,14},{2,13},{3,12},{4,11},{5,10},{6,9},{7,8},{8,7},{9,6},... | collective-permute-start | bytes 589832 | tf_op jit(solution)/shard_map/ppermute | solution.py:26
  392.1 13.2 %collective-permute-done.19 = bf16[1,48,2048]{2,1,0:T(8,128)(2,1)S(1)} collective-permute-done((bf16[1,48,2048]{2,1,0:T(8,128)(2,1)}, bf16[1,48,2048]{2,1,0:T(8,128)(2,1)S(1)}, u32[]{:S(2)}, u32[]{:S(2)}) %collective-permute-start.19) | collective-permute-done | bytes 196640 | tf_op jit(solution)/shard_map/ppermute | solution.py:26
  406.0 4.4 collective-permute-done.20
  411.1 3.2 collective-permute-done.21
  415.0 3.9 collective-permute-done.22
  419.6 4.3 gather_fusion
  424.0 4.3 convolution_reduce_fusion
  431.0 4.5 %multiply_reduce_fusion = f32[64,2048]{1,0:T(8,128)S(1)} fusion(bf16[768,2048,1]{1,0,2:T(8,128)(2,1)} %bitcast.31, f32[64,8]{1,0:T(8,128)S(1)} %copy-done.9, s32[64,8]{1,0:T(8,128)S(1)} %copy-done.7), kind=kOutput, calls=%fused_computation.10 | convolution fusion | flops 1612972032 | bytes 3674112 | tf_op jit(solution)/shard_map/dot_general | solution.py:96
  (146 shorter events, 89.3 us)
Async XLA Ops:
  0.6 224.9 %copy-start = (bf16[1,1,2048,768]{3,2,1,0:T(8,128)(2,1)S(1)}, bf16[1,1,2048,768]{3,2,1,0:T(8,128)(2,1)}, u32[]{:S(2)}) copy-start(bf16[1,1,2048,768]{3,2,1,0:T(8,128)(2,1)} %param.20) | copy-start | bytes 9437188
  14.9 19.1 %collective-permute-start = (bf16[64,6272]{1,0:T(8,128)(2,1)}, bf16[64,6272]{1,0:T(8,128)(2,1)}, u32[]{:S(2)}, u32[]{:S(2)}) collective-permute-start(bf16[64,6272]{1,0:T(8,128)(2,1)} %concatenate.11), channel_id=1, source_target_pairs={{0,4},{1,5},{2,6},{3,7},{4,8},{5,9},{6,10},{7,11},{8,12},{9,13},{1... | collective-permute-start | bytes 2408456 | tf_op jit(solution)/shard_map/ppermute | solution.py:123
  16.2 68.5 %collective-permute-start.1 = (bf16[64,6272]{1,0:T(8,128)(2,1)}, bf16[64,6272]{1,0:T(8,128)(2,1)}, u32[]{:S(2)}, u32[]{:S(2)}) collective-permute-start(bf16[64,6272]{1,0:T(8,128)(2,1)} %concatenate.11), channel_id=1, source_target_pairs={{0,8},{1,9},{2,10},{3,11},{4,12},{5,13},{6,14},{7,15},{8,0},{9,1},... | collective-permute-start | bytes 2408456 | tf_op jit(solution)/shard_map/ppermute | solution.py:123
  17.3 70.3 %collective-permute-start.2 = (bf16[64,6272]{1,0:T(8,128)(2,1)}, bf16[64,6272]{1,0:T(8,128)(2,1)}, u32[]{:S(2)}, u32[]{:S(2)}) collective-permute-start(bf16[64,6272]{1,0:T(8,128)(2,1)} %concatenate.11), channel_id=1, source_target_pairs={{0,12},{1,13},{2,14},{3,15},{4,0},{5,1},{6,2},{7,3},{8,4},{9,5},{1... | collective-permute-start | bytes 2408456 | tf_op jit(solution)/shard_map/ppermute | solution.py:123
  89.6 70.6 %collective-permute-start.3 = (bf16[4,64,6272]{2,1,0:T(8,128)(2,1)}, bf16[4,64,6272]{2,1,0:T(8,128)(2,1)}, u32[]{:S(2)}, u32[]{:S(2)}) collective-permute-start(bf16[4,64,6272]{2,1,0:T(8,128)(2,1)} %bitcast_dynamic-update-slice_fusion.3), channel_id=1, source_target_pairs={{0,1},{1,0},{2,3},{3,2},{4,5},{5,4},{6,7},{7,6},{8,9},{9,8},{10,11... | collective-permute-start | bytes 9633800 | tf_op jit(solution)/shard_map/ppermute | solution.py:127
  90.8 71.2 %collective-permute-start.4 = (bf16[4,64,6272]{2,1,0:T(8,128)(2,1)}, bf16[4,64,6272]{2,1,0:T(8,128)(2,1)}, u32[]{:S(2)}, u32[]{:S(2)}) collective-permute-start(bf16[4,64,6272]{2,1,0:T(8,128)(2,1)} %bitcast_dynamic-update-slice_fusion.3), channel_id=1, source_target_pairs={{0,2},{1,3},{2,0},{3,1},{4,6},{5,7},{6,4},{7,5},{8,10},{9,11},{10,... | collective-permute-start | bytes 9633800 | tf_op jit(solution)/shard_map/ppermute | solution.py:128
  161.7 35.0 %collective-permute-start.5 = (bf16[4,32,6272]{2,1,0:T(8,128)(2,1)S(1)}, bf16[4,32,6272]{2,1,0:T(8,128)(2,1)S(1)}, u32[]{:S(2)}, u32[]{:S(2)}) collective-permute-start(bf16[4,32,6272]{2,1,0:T(8,128)(2,1)S(1)} %slice.67), channel_id=1, source_target_pairs={{0,2},{1,3},{2,0},{3,1},{4,6},{5,7},{6,4},{7,5},{8,10},{9,11},{10,... | collective-permute-start | bytes 4816904 | tf_op jit(solution)/shard_map/ppermute | solution.py:130
  163.5 34.8 %collective-permute-start.6 = (bf16[4,32,6272]{2,1,0:T(8,128)(2,1)S(1)}, bf16[4,32,6272]{2,1,0:T(8,128)(2,1)S(1)}, u32[]{:S(2)}, u32[]{:S(2)}) collective-permute-start(bf16[4,32,6272]{2,1,0:T(8,128)(2,1)S(1)} %slice.68), channel_id=1, source_target_pairs={{0,1},{1,0},{2,3},{3,2},{4,5},{5,4},{6,7},{7,6},{8,9},{9,8},{10,11... | collective-permute-start | bytes 4816904 | tf_op jit(solution)/shard_map/ppermute | solution.py:131
  213.0 8.5 %copy-start.3 = (bf16[16,48,2048]{2,1,0:T(8,128)(2,1)}, bf16[16,48,2048]{2,1,0:T(8,128)(2,1)S(1)}, u32[]{:S(2)}) copy-start(bf16[16,48,2048]{2,1,0:T(8,128)(2,1)S(1)} %fusion.13) | copy-start | bytes 9437188
  246.3 33.8 %collective-permute-start.8 = (bf16[1,48,2048]{2,1,0:T(8,128)(2,1)}, bf16[1,48,2048]{2,1,0:T(8,128)(2,1)}, u32[]{:S(2)}, u32[]{:S(2)}) collective-permute-start(bf16[1,48,2048]{2,1,0:T(8,128)(2,1)} %get-tuple-element.18), channel_id=1, source_target_pairs={{0,1},{1,0},{2,3},{3,2},{4,5},{5,4},{6,7},{7,6},{8,9},{9,8},{10,11... | collective-permute-start | bytes 589832 | tf_op jit(solution)/shard_map/ppermute | solution.py:26
  247.5 34.8 %collective-permute-start.9 = (bf16[1,48,2048]{2,1,0:T(8,128)(2,1)}, bf16[1,48,2048]{2,1,0:T(8,128)(2,1)}, u32[]{:S(2)}, u32[]{:S(2)}) collective-permute-start(bf16[1,48,2048]{2,1,0:T(8,128)(2,1)} %get-tuple-element.17), channel_id=1, source_target_pairs={{0,2},{1,3},{2,0},{3,1},{4,6},{5,7},{6,4},{7,5},{8,10},{9,11},{10,... | collective-permute-start | bytes 589832 | tf_op jit(solution)/shard_map/ppermute | solution.py:26
  248.8 38.0 %collective-permute-start.10 = (bf16[1,48,2048]{2,1,0:T(8,128)(2,1)}, bf16[1,48,2048]{2,1,0:T(8,128)(2,1)}, u32[]{:S(2)}, u32[]{:S(2)}) collective-permute-start(bf16[1,48,2048]{2,1,0:T(8,128)(2,1)} %get-tuple-element.16), channel_id=1, source_target_pairs={{0,3},{1,2},{2,1},{3,0},{4,7},{5,6},{6,5},{7,4},{8,11},{9,10},{10,... | collective-permute-start | bytes 589832 | tf_op jit(solution)/shard_map/ppermute | solution.py:26
  248.9 41.5 %collective-permute-start.11 = (bf16[1,48,2048]{2,1,0:T(8,128)(2,1)}, bf16[1,48,2048]{2,1,0:T(8,128)(2,1)}, u32[]{:S(2)}, u32[]{:S(2)}) collective-permute-start(bf16[1,48,2048]{2,1,0:T(8,128)(2,1)} %get-tuple-element.15), channel_id=1, source_target_pairs={{0,4},{1,5},{2,6},{3,7},{4,0},{5,1},{6,2},{7,3},{8,12},{9,13},{10,... | collective-permute-start | bytes 589832 | tf_op jit(solution)/shard_map/ppermute | solution.py:26
  249.0 43.4 %collective-permute-start.12 = (bf16[1,48,2048]{2,1,0:T(8,128)(2,1)}, bf16[1,48,2048]{2,1,0:T(8,128)(2,1)}, u32[]{:S(2)}, u32[]{:S(2)}) collective-permute-start(bf16[1,48,2048]{2,1,0:T(8,128)(2,1)} %get-tuple-element.14), channel_id=1, source_target_pairs={{0,5},{1,4},{2,7},{3,6},{4,1},{5,0},{6,3},{7,2},{8,13},{9,12},{10,... | collective-permute-start | bytes 589832 | tf_op jit(solution)/shard_map/ppermute | solution.py:26
  274.9 156.1 %all-to-all-start = ((bf16[16,48,2048]{2,1,0:T(8,128)(2,1)}), bf16[16,48,2048]{2,1,0:T(8,128)(2,1)}, u32[]{:S(2)}, u32[]{:S(2)}) async-start(bf16[16,48,2048]{2,1,0:T(8,128)(2,1)} %bitcast.251), calls=%async_computation | async-start | bytes 6291456 | tf_op jit(solution)/shard_map/all_to_all | solution.py:197
  280.1 54.5 %collective-permute-start.13 = (bf16[1,48,2048]{2,1,0:T(8,128)(2,1)}, bf16[1,48,2048]{2,1,0:T(8,128)(2,1)S(1)}, u32[]{:S(2)}, u32[]{:S(2)}) collective-permute-start(bf16[1,48,2048]{2,1,0:T(8,128)(2,1)} %get-tuple-element.13), channel_id=1, source_target_pairs={{0,6},{1,7},{2,4},{3,5},{4,2},{5,3},{6,0},{7,1},{8,14},{9,15},{10,... | collective-permute-start | bytes 589832 | tf_op jit(solution)/shard_map/ppermute | solution.py:26
  282.3 56.0 %collective-permute-start.14 = (bf16[1,48,2048]{2,1,0:T(8,128)(2,1)}, bf16[1,48,2048]{2,1,0:T(8,128)(2,1)S(1)}, u32[]{:S(2)}, u32[]{:S(2)}) collective-permute-start(bf16[1,48,2048]{2,1,0:T(8,128)(2,1)} %get-tuple-element.12), channel_id=1, source_target_pairs={{0,7},{1,6},{2,5},{3,4},{4,3},{5,2},{6,1},{7,0},{8,15},{9,14},{10,... | collective-permute-start | bytes 589832 | tf_op jit(solution)/shard_map/ppermute | solution.py:26
  286.7 83.9 %collective-permute-start.15 = (bf16[1,48,2048]{2,1,0:T(8,128)(2,1)}, bf16[1,48,2048]{2,1,0:T(8,128)(2,1)S(1)}, u32[]{:S(2)}, u32[]{:S(2)}) collective-permute-start(bf16[1,48,2048]{2,1,0:T(8,128)(2,1)} %get-tuple-element.11), channel_id=1, source_target_pairs={{0,8},{1,9},{2,10},{3,11},{4,12},{5,13},{6,14},{7,15},{8,0},{9,1},... | collective-permute-start | bytes 589832 | tf_op jit(solution)/shard_map/ppermute | solution.py:26
  290.5 85.2 %collective-permute-start.16 = (bf16[1,48,2048]{2,1,0:T(8,128)(2,1)}, bf16[1,48,2048]{2,1,0:T(8,128)(2,1)S(1)}, u32[]{:S(2)}, u32[]{:S(2)}) collective-permute-start(bf16[1,48,2048]{2,1,0:T(8,128)(2,1)} %get-tuple-element.10), channel_id=1, source_target_pairs={{0,9},{1,8},{2,11},{3,10},{4,13},{5,12},{6,15},{7,14},{8,1},{9,0},... | collective-permute-start | bytes 589832 | tf_op jit(solution)/shard_map/ppermute | solution.py:26
  292.3 88.9 %collective-permute-start.17 = (bf16[1,48,2048]{2,1,0:T(8,128)(2,1)}, bf16[1,48,2048]{2,1,0:T(8,128)(2,1)S(1)}, u32[]{:S(2)}, u32[]{:S(2)}) collective-permute-start(bf16[1,48,2048]{2,1,0:T(8,128)(2,1)} %get-tuple-element.9), channel_id=1, source_target_pairs={{0,10},{1,11},{2,8},{3,9},{4,14},{5,15},{6,12},{7,13},{8,2},{9,3},... | collective-permute-start | bytes 589832 | tf_op jit(solution)/shard_map/ppermute | solution.py:26
  334.6 56.7 %collective-permute-start.18 = (bf16[1,48,2048]{2,1,0:T(8,128)(2,1)}, bf16[1,48,2048]{2,1,0:T(8,128)(2,1)S(1)}, u32[]{:S(2)}, u32[]{:S(2)}) collective-permute-start(bf16[1,48,2048]{2,1,0:T(8,128)(2,1)} %get-tuple-element.8), channel_id=1, source_target_pairs={{0,11},{1,10},{2,9},{3,8},{4,15},{5,14},{6,13},{7,12},{8,3},{9,2},... | collective-permute-start | bytes 589832 | tf_op jit(solution)/shard_map/ppermute | solution.py:26
  338.3 67.0 %collective-permute-start.19 = (bf16[1,48,2048]{2,1,0:T(8,128)(2,1)}, bf16[1,48,2048]{2,1,0:T(8,128)(2,1)S(1)}, u32[]{:S(2)}, u32[]{:S(2)}) collective-permute-start(bf16[1,48,2048]{2,1,0:T(8,128)(2,1)} %get-tuple-element.7), channel_id=1, source_target_pairs={{0,12},{1,13},{2,14},{3,15},{4,8},{5,9},{6,10},{7,11},{8,4},{9,5},... | collective-permute-start | bytes 589832 | tf_op jit(solution)/shard_map/ppermute | solution.py:26
  370.6 39.7 %collective-permute-start.20 = (bf16[1,48,2048]{2,1,0:T(8,128)(2,1)}, bf16[1,48,2048]{2,1,0:T(8,128)(2,1)S(1)}, u32[]{:S(2)}, u32[]{:S(2)}) collective-permute-start(bf16[1,48,2048]{2,1,0:T(8,128)(2,1)} %get-tuple-element.6), channel_id=1, source_target_pairs={{0,13},{1,12},{2,15},{3,14},{4,9},{5,8},{6,11},{7,10},{8,5},{9,4},... | collective-permute-start | bytes 589832 | tf_op jit(solution)/shard_map/ppermute | solution.py:26
  375.7 38.6 %collective-permute-start.21 = (bf16[1,48,2048]{2,1,0:T(8,128)(2,1)S(1)}, bf16[1,48,2048]{2,1,0:T(8,128)(2,1)S(1)}, u32[]{:S(2)}, u32[]{:S(2)}) collective-permute-start(bf16[1,48,2048]{2,1,0:T(8,128)(2,1)S(1)} %get-tuple-element.5), channel_id=1, source_target_pairs={{0,14},{1,15},{2,12},{3,13},{4,10},{5,11},{6,8},{7,9},{8,6},{9,7},... | collective-permute-start | bytes 589832 | tf_op jit(solution)/shard_map/ppermute | solution.py:26
  381.2 37.8 %collective-permute-start.22 = (bf16[1,48,2048]{2,1,0:T(8,128)(2,1)S(1)}, bf16[1,48,2048]{2,1,0:T(8,128)(2,1)S(1)}, u32[]{:S(2)}, u32[]{:S(2)}) collective-permute-start(bf16[1,48,2048]{2,1,0:T(8,128)(2,1)S(1)} %get-tuple-element.4), channel_id=1, source_target_pairs={{0,15},{1,14},{2,13},{3,12},{4,11},{5,10},{6,9},{7,8},{8,7},{9,6},... | collective-permute-start | bytes 589832 | tf_op jit(solution)/shard_map/ppermute | solution.py:26
  424.0 4.6 %copy-start.6 = (bf16[1,64,2048]{2,1,0:T(8,128)(2,1)S(1)}, bf16[1,64,2048]{2,1,0:T(8,128)(2,1)}, u32[]{:S(2)}) copy-start(bf16[1,64,2048]{2,1,0:T(8,128)(2,1)} %param.15) | copy-start | bytes 786436
  424.0 4.6 %copy-start.11 = (f32[64]{0:T(128)S(1)}, f32[64]{0:T(128)}, u32[]{:S(2)}) copy-start(f32[64]{0:T(128)} %copy-done.10) | copy-start | bytes 772
  424.0 4.6 %copy-start.12 = (f32[64]{0:T(128)S(1)}, f32[64]{0:T(128)}, u32[]{:S(2)}) copy-start(f32[64]{0:T(128)} %get-tuple-element.29) | copy-start | bytes 772
  424.0 7.0 %copy-start.7 = (s32[64,8]{1,0:T(8,128)S(1)}, s32[64,8]{1,0:T(8,128)}, u32[]{:S(2)}) copy-start(s32[64,8]{1,0:T(8,128)} %bitcast_add_fusion.1) | copy-start | bytes 6148
  424.0 7.0 %copy-start.9 = (f32[64,8]{1,0:T(8,128)S(1)}, f32[64,8]{1,0:T(8,128)}, u32[]{:S(2)}) copy-start(f32[64,8]{1,0:T(8,128)} %copy.37) | copy-start | bytes 6148
  429.6 6.1 %collective-permute-start.23 = (bf16[1,64,2048]{2,1,0:T(8,128)(2,1)}, bf16[1,64,2048]{2,1,0:T(8,128)(2,1)S(1)}, u32[]{:S(2)}, u32[]{:S(2)}) collective-permute-start(bf16[1,64,2048]{2,1,0:T(8,128)(2,1)} %fusion.66), channel_id=1, source_target_pairs={{16,0},{0,16},{17,1},{1,17},{18,2},{2,18},{19,3},{3,19},{20,4},{4,... | collective-permute-start | bytes 786440 | tf_op jit(solution)/shard_map/ppermute | solution.py:34
  435.5 1.6 collective-permute-start.7
  (8 other events, 25.8 us)
